TPU v7x, 512 devices: a whole 4x4x16 slice. The times are simulated.
512 devices in a mesh: dp: 8 (over x, core), expert: 64 (over y, z).
Axes of the slice: x: 4, y: 4, z: 16, core: 2. Of those that a mesh axis runs over, the one named last changes fastest.
Arguments:
- tokens: bfloat16 [65536, 1024], P(('dp', 'expert')), may hold values from -6 to 6
- grad_out: bfloat16 [65536, 1024], P(('dp', 'expert')), may hold values from -6 to 6
- expert_ids: int32 [65536, 8], P(('dp', 'expert')), may hold values from 0 to 63, all different within a row; in each aligned block of 128 rows (0 to 127, 128 to 255, ...) at most 18 rows name the same one
- gates: float32 [65536, 8], P(('dp', 'expert')), may hold values from 0.1 to 0.5
- w_in: bfloat16 [64, 1024, 768], P('expert', 'dp'), may hold values from -0.1875 to 0.1875
- w_down: bfloat16 [64, 384, 1024], P('expert', 'dp'), may hold values from -0.3125 to 0.3125
Outputs:
- grad_tokens: bfloat16 [65536, 1024], P(('dp', 'expert'))
- grad_in: float32 [64, 1024, 768], P('expert', 'dp')
- grad_down: float32 [64, 384, 1024], P('expert', 'dp')
Inputs may be any that keep to these rules, and one draw needn't show every extreme that they name: `expert_ids`: each token names 8 different experts; among the tokens of one device no expert is named more than 18 times, a bound that some block reaches.
All inputs are finite; a program needn't handle non-finite values.
Results may differ from a plain program's by a relative error of at most 0.015.
Values may be sent and summed in bfloat16 or wider, within the bound.
No kernel may reach another device: no remote copies, remote signals or barrier semaphores. Data moves between devices by JAX's collectives and lax.ppermute only.
A program may use at most 64 MiB of HBM per device.

v0:
```python
import jax
import jax.numpy as jnp
from jax import lax
from jax.sharding import PartitionSpec as P


def hidden_from(preact):
    half_width = preact.shape[1] // 2
    gate_pre = preact[:, :half_width]
    up_pre = preact[:, half_width:]
    sigmoid_gate = jax.nn.sigmoid(gate_pre)
    return (gate_pre * sigmoid_gate * up_pre).astype(jnp.bfloat16)


def pre_grads(preact, grad_hidden):
    half_width = preact.shape[1] // 2
    gate_pre = preact[:, :half_width]
    up_pre = preact[:, half_width:]
    sigmoid_gate = jax.nn.sigmoid(gate_pre)
    grad_gate = grad_hidden * up_pre * sigmoid_gate * (1.0 + gate_pre * (1.0 - sigmoid_gate))
    grad_up = grad_hidden * gate_pre * sigmoid_gate
    return jnp.concatenate([grad_gate, grad_up], axis=1).astype(jnp.bfloat16)


def contract_first(left, right):
    return lax.dot_general(
        left, right, (((0,), (0,)), ((), ())), preferred_element_type=jnp.float32
    )


def contract_last(left, right):
    return lax.dot_general(
        left, right, (((1,), (1,)), ((), ())), preferred_element_type=jnp.float32
    )


def expert_exchange(slots, expert_count):
    slot_total, chunks, lanes = slots.shape
    blocks = slots.reshape(expert_count, slot_total // expert_count * chunks, lanes)
    blocks = lax.all_to_all(blocks, "expert", 0, 0, tiled=True)
    return blocks.reshape(slot_total, chunks, lanes)


def on_device(tokens, grad_out, expert_ids, gates, w_in, w_down):
    token_rows, model_width = tokens.shape
    route_width = expert_ids.shape[1]
    expert_count = lax.axis_size("expert")
    route_total = token_rows * route_width
    capacity = route_total // expert_count + max(1, route_total // (8 * expert_count))
    slot_total = expert_count * capacity
    flat_ids = expert_ids.reshape(route_total)
    route_marks = (flat_ids[:, None] == jnp.arange(expert_count, dtype=jnp.int32)[None, :]).astype(
        jnp.int32
    )
    route_index = jnp.arange(route_total, dtype=jnp.int32)
    lower_table = (route_index[None, :] <= route_index[:, None]).astype(jnp.bfloat16)
    running = jnp.dot(
        lower_table, route_marks.astype(jnp.bfloat16), preferred_element_type=jnp.float32
    )
    slot_ranks = jnp.sum((running.astype(jnp.int32) - 1) * route_marks, axis=1)
    targets = flat_ids * capacity + slot_ranks
    slot_index = jnp.arange(slot_total, dtype=jnp.int32)
    slot_hits = slot_index[:, None] == targets[None, :]
    slot_gates = jnp.sum(jnp.where(slot_hits, gates.reshape(route_total)[None, :], 0.0), axis=1)
    token_of_route = (
        route_index[:, None] // route_width == jnp.arange(token_rows, dtype=jnp.int32)[None, :]
    ).astype(jnp.bfloat16)
    slot_of_token = jnp.dot(
        slot_hits.astype(jnp.bfloat16), token_of_route, preferred_element_type=jnp.float32
    ).astype(jnp.bfloat16)
    chunks = model_width // 128
    both_rows = jnp.concatenate(
        [tokens.reshape(token_rows, chunks, 128), grad_out.reshape(token_rows, chunks, 128)], axis=1
    )
    slot_routes = jnp.sum(jnp.where(slot_hits, route_index[None, :], 0), axis=1)
    occupied = jnp.any(slot_hits, axis=1)
    picked = both_rows[slot_routes // route_width].astype(jnp.float32)
    chunk_index = jnp.arange(2 * chunks, dtype=jnp.int32)[None, :, None]
    row_scale = jnp.where(
        chunk_index < chunks, jnp.ones((), jnp.float32), slot_gates[:, None, None]
    )
    row_scale = jnp.where(occupied[:, None, None], row_scale, jnp.zeros((), jnp.float32))
    send_both = (row_scale * picked).astype(jnp.bfloat16)
    recv_both = expert_exchange(send_both, expert_count)
    slot_tokens = recv_both[:, :chunks, :].reshape(slot_total, model_width)
    slot_grads = recv_both[:, chunks:, :].reshape(slot_total, model_width)
    local_in = w_in[0]
    local_down = w_down[0]
    full_in, full_down = (
        lax.all_gather(local_in, "dp", axis=0, tiled=True),
        lax.all_gather(local_down, "dp", axis=0, tiled=True),
    )
    preact = jnp.dot(slot_tokens, full_in, preferred_element_type=jnp.float32)
    grad_hidden = contract_last(slot_grads, full_down)
    pre_grad = pre_grads(preact, grad_hidden)
    slot_back = (
        contract_last(pre_grad, full_in).astype(jnp.bfloat16).reshape(slot_total, chunks, 128)
    )
    hidden_act = hidden_from(preact)
    grad_in_local = lax.psum_scatter(
        contract_first(slot_tokens, pre_grad).astype(jnp.bfloat16),
        "dp",
        scatter_dimension=0,
        tiled=True,
    ).astype(jnp.float32)
    grad_down_local = lax.psum_scatter(
        contract_first(hidden_act, slot_grads).astype(jnp.bfloat16),
        "dp",
        scatter_dimension=0,
        tiled=True,
    ).astype(jnp.float32)
    slot_return = expert_exchange(slot_back, expert_count)
    grad_tokens = (
        contract_first(slot_of_token, slot_return)
        .astype(jnp.bfloat16)
        .reshape(token_rows, model_width)
    )
    return (grad_tokens, grad_in_local[None], grad_down_local[None])


def solution(mesh):
    token_spec = P(("dp", "expert"), None)
    weight_spec = P("expert", "dp", None)
    in_specs = (token_spec, token_spec, token_spec, token_spec, weight_spec, weight_spec)
    out_specs = (token_spec, weight_spec, weight_spec)
    return jax.shard_map(
        on_device, mesh=mesh, in_specs=in_specs, out_specs=out_specs, check_vma=False
    )
```

profile of v0, /device:TPU:38, one launch (start us, length us, event | category | flops | bytes accessed | tf_op | source)
XLA Modules:
  0.0 400.0 jit_solution(4009378944013035038)
XLA Ops:
  7.2 0.8 copy.18
  10.2 0.8 copy.20
  12.7 4.8 %gather_fusion = bf16[1152,16,128]{2,1,0:T(8,128)(2,1)} fusion(bf16[128,16,128]{2,1,0:T(8,128)(2,1)S(1)} %pad_maximum_fusion.3, s32[2048]{0:T(1024)S(1)} %pad_clamp_fusion), kind=kCustom, calls=%fused_computation | custom fusion | bytes 9441792 | tf_op jit(solution)/shard_map/gather | solution.py:77
  17.5 6.3 %fusion = bf16[64,288,128]{2,1,0:T(8,128)(2,1)} fusion(f32[64,288]{1,0:T(8,128)S(1)} %copy.23, bf16[64,288,128]{2,1,0:T(8,128)(2,1)} %bitcast.56), kind=kLoop, calls=%fused_computation.2 | loop fusion | flops 7077888 | bytes 9510912 | tf_op jit(solution)/shard_map/convert_element_type | solution.py:83
  23.8 18.7 %all-to-all-start = ((bf16[64,288,128]{2,1,0:T(8,128)(2,1)}), bf16[64,288,128]{2,1,0:T(8,128)(2,1)}, u32[]{:S(2)}, u32[]{:S(2)}) async-start(bf16[64,288,128]{2,1,0:T(8,128)(2,1)} %fusion), calls=%async_computation | async-start | bytes 9437184 | tf_op jit(solution)/shard_map/all_to_all | solution.py:40
  43.2 13.6 %all-gather = bf16[1,384,1024]{2,1,0:T(8,128)(2,1)S(1)} all-gather(bf16[1,48,1024]{2,1,0:T(8,128)(2,1)S(1)} %copy-done.4), channel_id=2, replica_groups=mesh['dp'=8,'expert'=64] {'dp'}, dimensions={1}, use_global_device_ids=true | all-gather | bytes 884736 | tf_op jit(solution)/shard_map/all_gather | solution.py:91
  56.8 194.9 %all-to-all-done = bf16[64,288,128]{2,1,0:T(8,128)(2,1)} async-done(((bf16[64,288,128]{2,1,0:T(8,128)(2,1)}), bf16[64,288,128]{2,1,0:T(8,128)(2,1)}, u32[]{:S(2)}, u32[]{:S(2)}) %all-to-all-start) | async-done | bytes 4718624 | tf_op jit(solution)/shard_map/all_to_all | solution.py:40
  251.7 3.6 fusion.44
  255.4 4.7 %fusion.7 = f32[1152,768]{0,1:T(8,128)S(1)} fusion(bf16[144,8,8,128]{3,2,1,0:T(8,128)(2,1)S(1)} %bitcast.59, bf16[1,1024,768]{2,1,0:T(8,128)(2,1)} %all-gather.4.cloned.1.call-done), kind=kOutput, calls=%fused_computation.14 | convolution fusion | flops 1811939328 | bytes 7471104 | tf_op jit(solution)/shard_map/dot_general | solution.py:93
  260.1 1.7 multiply_convert_fusion.2
  261.9 0.9 copy-done.7
  263.1 2.1 convolution_convert_fusion
  265.1 2.5 reshape_reshape.3
  267.6 8.7 %all-to-all-start.1 = ((bf16[64,144,128]{2,1,0:T(8,128)(2,1)}), bf16[64,144,128]{2,1,0:T(8,128)(2,1)S(1)}, u32[]{:S(2)}, u32[]{:S(2)}) async-start(bf16[64,144,128]{2,1,0:T(8,128)(2,1)} %reshape_reshape.3), calls=%async_computation.1 | async-start | bytes 4718592 | tf_op jit(solution)/shard_map/all_to_all | solution.py:40
  276.3 4.9 %fusion.23 = bf16[384,1024]{1,0:T(8,128)(2,1)} fusion(bf16[144,8,8,128]{3,2,1,0:T(8,128)(2,1)} %bitcast.61, f32[1152,768]{0,1:T(8,128)} %copy-done.6), kind=kOutput, calls=%fused_computation.33 | convolution fusion | flops 909017088 | bytes 6684672 | tf_op jit(solution)/shard_map/dot_general | solution.py:26
  281.6 5.6 %fusion.18 = bf16[1024,768]{1,0:T(8,128)(2,1)} fusion(bf16[144,8,8,128]{3,2,1,0:T(8,128)(2,1)} %bitcast.60, bf16[1152,384]{0,1:T(8,128)(2,1)} %copy-done.8, bf16[1152,384]{0,1:T(8,128)(2,1)} %copy-done.7), kind=kOutput, calls=%fused_computation.30 | convolution fusion | flops 1816264704 | bytes 5701632 | tf_op jit(solution)/shard_map/dot_general | solution.py:26
  287.1 31.9 %reduce-scatter.5.cloned.1.call-done = bf16[48,1024]{1,0:T(8,128)(2,1)} async-done(((bf16[384,1024]{1,0:T(8,128)(2,1)}), bf16[48,1024]{1,0:T(8,128)(2,1)}) %reduce-scatter.5.cloned.1.call-update) | async-done | bytes 98320 | tf_op jit(solution)/shard_map/reduce_scatter | solution.py:106
  319.0 1.6 bitcast_convert_fusion.1
  320.6 41.5 %reduce-scatter.3.cloned.1.call-done = bf16[128,768]{1,0:T(8,128)(2,1)} async-done(((bf16[1024,768]{1,0:T(8,128)(2,1)}), bf16[128,768]{1,0:T(8,128)(2,1)}) %reduce-scatter.3.cloned.1.call-update) | async-done | bytes 196624 | tf_op jit(solution)/shard_map/reduce_scatter | solution.py:100
  362.1 1.7 bitcast_convert_fusion
  363.8 21.8 %all-to-all-done.1 = bf16[64,144,128]{2,1,0:T(8,128)(2,1)S(1)} async-done(((bf16[64,144,128]{2,1,0:T(8,128)(2,1)}), bf16[64,144,128]{2,1,0:T(8,128)(2,1)S(1)}, u32[]{:S(2)}, u32[]{:S(2)}) %all-to-all-start.1) | async-done | bytes 2359328 | tf_op jit(solution)/shard_map/all_to_all | solution.py:40
  385.6 2.8 copy.24
  388.3 4.2 %fusion.26 = f32[128,1024]{0,1:S(1)} fusion(bf16[1152,1024]{0,1:T(8,128)(2,1)} %bitcast.58, s32[1024]{0:T(1024)S(1)} %get-tuple-element.17, s32[1024]{0:T(1024)S(1)} %get-tuple-element.16), kind=kOutput, calls=%fused_computation.34 | convolution fusion | flops 605437952 | bytes 2891776
  392.6 0.9 copy.25
  (47 shorter events, 5.3 us)
Async XLA Ops:
  7.2 5.3 %copy-start.2 = (bf16[128,1024]{1,0:T(8,128)(2,1)S(1)}, bf16[128,1024]{1,0:T(8,128)(2,1)}, u32[]{:S(2)}) copy-start(bf16[128,1024]{1,0:T(8,128)(2,1)} %param.6) | copy-start | bytes 786436
  7.2 5.4 %copy-start.3 = (bf16[128,1024]{1,0:T(8,128)(2,1)S(1)}, bf16[128,1024]{1,0:T(8,128)(2,1)}, u32[]{:S(2)}) copy-start(bf16[128,1024]{1,0:T(8,128)(2,1)} %param.7) | copy-start | bytes 786436
  23.8 19.4 %copy-start.4 = (bf16[1,48,1024]{2,1,0:T(8,128)(2,1)S(1)}, bf16[1,48,1024]{2,1,0:T(8,128)(2,1)}, u32[]{:S(2)}) copy-start(bf16[1,48,1024]{2,1,0:T(8,128)(2,1)} %param.11) | copy-start | bytes 294916
  23.8 227.9 %all-to-all-start = ((bf16[64,288,128]{2,1,0:T(8,128)(2,1)}), bf16[64,288,128]{2,1,0:T(8,128)(2,1)}, u32[]{:S(2)}, u32[]{:S(2)}) async-start(bf16[64,288,128]{2,1,0:T(8,128)(2,1)} %fusion), calls=%async_computation | async-start | bytes 9437184 | tf_op jit(solution)/shard_map/all_to_all | solution.py:40
  42.5 212.9 %all-gather.4.cloned.1.call-start = ((), (), s32[]{:S(2)}) async-start(), calls=%async_computation.6 | async-start | bytes 1769472 | tf_op jit(solution)/shard_map/all_gather | solution.py:90
  255.3 4.7 %copy-start = (bf16[1152,8,128]{2,1,0:T(8,128)(2,1)}, bf16[1152,8,128]{2,1,0:T(8,128)(2,1)S(1)}, u32[]{:S(2)}) copy-start(bf16[1152,8,128]{2,1,0:T(8,128)(2,1)S(1)} %get-tuple-element.14) | copy-start | bytes 7077892
  255.4 4.7 %copy-start.1 = (bf16[1152,8,128]{2,1,0:T(8,128)(2,1)S(1)}, bf16[1152,8,128]{2,1,0:T(8,128)(2,1)}, u32[]{:S(2)}) copy-start(bf16[1152,8,128]{2,1,0:T(8,128)(2,1)} %get-tuple-element.15) | copy-start | bytes 7077892
  260.0 1.8 copy-start.6
  260.1 3.0 copy-start.5
  261.9 0.9 copy-start.7
  261.9 1.2 copy-start.8
  267.6 117.9 %all-to-all-start.1 = ((bf16[64,144,128]{2,1,0:T(8,128)(2,1)}), bf16[64,144,128]{2,1,0:T(8,128)(2,1)S(1)}, u32[]{:S(2)}, u32[]{:S(2)}) async-start(bf16[64,144,128]{2,1,0:T(8,128)(2,1)} %reshape_reshape.3), calls=%async_computation.1 | async-start | bytes 4718592 | tf_op jit(solution)/shard_map/all_to_all | solution.py:40
  276.3 42.7 %reduce-scatter.5.cloned.1.call-start = ((), (), s32[]{:S(2)}) async-start(), calls=%async_computation.5 | async-start | bytes 884736 | tf_op jit(solution)/shard_map/reduce_scatter | solution.py:106
  281.3 80.8 %reduce-scatter.3.cloned.1.call-start = ((), (), s32[]{:S(2)}) async-start(), calls=%async_computation.4 | async-start | bytes 1769472 | tf_op jit(solution)/shard_map/reduce_scatter | solution.py:100
Sparse Core Ops, SparseCore 0:
  45.4 31.1 all-gather.3
  281.4 37.5 reduce-scatter.4
  321.9 40.1 reduce-scatter.2
where the time goes:
time: 400 us
  waiting for transfers between devices  291 us (73%)
  starting transfers between devices  27.7 us (7%)
  matrix products  23.7 us (6%)
  local copies, waits for them, and re-layouts  18.8 us (5%)
  between operations  14 us (4%)
  blocking collectives  13.6 us (3%)
  other arithmetic  11.5 us (3%)
    all_to_all x2, waiting for transfers between devices, expert_exchange(): blocks = lax.all_to_all(blocks, 'expert', 0, 0, tiled=True)  217 us
    reduce_scatter x1, waiting for transfers between devices, on_device(): lax.psum_scatter(contract_first(slot_tokens, pre_grad).astype(jnp.bfloat1...  41.5 us
    reduce_scatter x1, waiting for transfers between devices, on_device(): lax.psum_scatter(contract_first(hidden_act, slot_grads).astype(jnp.bfloat...  31.9 us
    all_to_all x2, starting transfers between devices, expert_exchange(): blocks = lax.all_to_all(blocks, 'expert', 0, 0, tiled=True)  27.3 us
    all_gather x1, blocking collectives, on_device(): lax.all_gather(local_down, 'dp', axis=0, tiled=True)  13.6 us
    dot_general x2, matrix products, contract_first(): lax.dot_general(left, right, (((0,), (0,)), ((), ())), preferred_element_...  10.5 us
  transfers between devices with their start and end apart: 5, of which 4 were waited for; matrix products, arithmetic and copies ran while one was open for 4% of the time, Pallas kernels for 0%

commit v1 on v0

--- a/solution.py
+++ b/solution.py
@@ -2,6 +2,11 @@
 import jax.numpy as jnp
 from jax import lax
 from jax.sharding import PartitionSpec as P
+
+
+def gather_from_all(x, axis, dim):
+    copies = jnp.concatenate([x] * lax.axis_size(axis), axis=dim)
+    return lax.all_to_all(copies, axis, dim, dim, tiled=True)
 
 
 def hidden_from(preact):
@@ -88,7 +93,7 @@
     local_down = w_down[0]
     full_in, full_down = (
         lax.all_gather(local_in, "dp", axis=0, tiled=True),
-        lax.all_gather(local_down, "dp", axis=0, tiled=True),
+        gather_from_all(local_down, "dp", 0),
     )
     preact = jnp.dot(slot_tokens, full_in, preferred_element_type=jnp.float32)
     grad_hidden = contract_last(slot_grads, full_down)

time: 400 us -> 412 us (1.030)
  the two profiles are of different devices: /device:TPU:38 before, /device:TPU:32 now
where the time goes in v1:
time: 412 us; the launch traced here: 411 us
  waiting for transfers between devices  302 us (73%)
  starting transfers between devices  32 us (8%)
  matrix products  28.1 us (7%)
  local copies, waits for them, and re-layouts  23.8 us (6%)
  between operations  13.9 us (3%)
  other arithmetic  11.5 us (3%)
    all_to_all x2, waiting for transfers between devices, expert_exchange(): blocks = lax.all_to_all(blocks, 'expert', 0, 0, tiled=True)  223 us
    reduce_scatter x1, waiting for transfers between devices, on_device(): lax.psum_scatter(contract_first(slot_tokens, pre_grad).astype(jnp.bfloat1...  41.7 us
    reduce_scatter x1, waiting for transfers between devices, on_device(): lax.psum_scatter(contract_first(hidden_act, slot_grads).astype(jnp.bfloat...  33.1 us
    all_to_all x2, starting transfers between devices, expert_exchange(): blocks = lax.all_to_all(blocks, 'expert', 0, 0, tiled=True)  27.3 us
    dot_general x2, matrix products, contract_first(): lax.dot_general(left, right, (((0,), (0,)), ((), ())), preferred_element_...  10.4 us
    unnamed x26, local copies, waits for them, and re-layouts  8.34 us
  transfers between devices with their start and end apart: 6, of which 5 were waited for; matrix products, arithmetic and copies ran while one was open for 7% of the time, Pallas kernels for 0%

profile of v1, /device:TPU:32, one launch (start us, length us, event | category | flops | bytes accessed | tf_op | source)
XLA Modules:
  0.0 411.4 jit_solution(5260838658396329920)
XLA Ops:
  7.2 0.8 copy.18
  12.7 4.8 %gather_fusion = bf16[1152,16,128]{2,1,0:T(8,128)(2,1)} fusion(bf16[128,16,128]{2,1,0:T(8,128)(2,1)S(1)} %pad_maximum_fusion.3, s32[2048]{0:T(1024)S(1)} %pad_clamp_fusion), kind=kCustom, calls=%fused_computation | custom fusion | bytes 9441792 | tf_op jit(solution)/shard_map/gather | solution.py:82
  17.5 6.2 %fusion = bf16[64,288,128]{2,1,0:T(8,128)(2,1)} fusion(f32[64,288]{1,0:T(8,128)S(1)} %copy.23, bf16[64,288,128]{2,1,0:T(8,128)(2,1)} %bitcast.63), kind=kLoop, calls=%fused_computation.2 | loop fusion | flops 7077888 | bytes 9510912 | tf_op jit(solution)/shard_map/convert_element_type | solution.py:88
  23.8 18.7 %all-to-all-start = ((bf16[64,288,128]{2,1,0:T(8,128)(2,1)}), bf16[64,288,128]{2,1,0:T(8,128)(2,1)}, u32[]{:S(2)}, u32[]{:S(2)}) async-start(bf16[64,288,128]{2,1,0:T(8,128)(2,1)} %fusion), calls=%async_computation | async-start | bytes 9437184 | tf_op jit(solution)/shard_map/all_to_all | solution.py:45
  48.4 203.3 %all-to-all-done = bf16[64,288,128]{2,1,0:T(8,128)(2,1)} async-done(((bf16[64,288,128]{2,1,0:T(8,128)(2,1)}), bf16[64,288,128]{2,1,0:T(8,128)(2,1)}, u32[]{:S(2)}, u32[]{:S(2)}) %all-to-all-start) | async-done | bytes 4718624 | tf_op jit(solution)/shard_map/all_to_all | solution.py:45
  251.7 4.3 %all-to-all-start.1 = ((bf16[8,48,1024]{2,1,0:T(8,128)(2,1)}), bf16[8,48,1024]{2,1,0:T(8,128)(2,1)S(1)}, u32[]{:S(2)}, u32[]{:S(2)}) async-start(bf16[8,48,1024]{2,1,0:T(8,128)(2,1)} %bitcast.5), calls=%async_computation.1 | async-start | bytes 1572864 | tf_op jit(solution)/shard_map/all_to_all | solution.py:9
  256.0 3.6 fusion.43
  259.6 6.4 %fusion.7 = f32[1152,768]{0,1:T(8,128)} fusion(bf16[144,8,8,128]{3,2,1,0:T(8,128)(2,1)S(1)} %bitcast.66, bf16[1,1024,768]{2,1,0:T(8,128)(2,1)} %all-gather.3.cloned.1.call-done), kind=kOutput, calls=%fused_computation.14 | convolution fusion | flops 1811939328 | bytes 7471104 | tf_op jit(solution)/shard_map/dot_general | solution.py:98
  266.1 3.1 all-to-all-done.1
  269.2 4.4 %multiply_convert_fusion.2 = (bf16[1152,384]{0,1:T(8,128)(2,1)S(1)}, bf16[1152,384]{0,1:T(8,128)(2,1)S(1)}) fusion(f32[1152,768]{0,1:T(8,128)} %fusion.7, bf16[384,1024]{1,0:T(8,128)(2,1)S(1)} %bitcast.73, bf16[144,8,8,128]{3,2,1,0:T(8,128)(2,1)} %bitcast.68), kind=kOutput, calls=%fused_computation.28 | convolution fusion | flops 911720448 | bytes 8454144 | tf_op jit(solution)/shard_map/dot_general | solution.py:37
  273.6 0.9 copy-done.5
  274.8 2.0 convolution_convert_fusion
  276.9 2.5 reshape_reshape.3
  279.4 8.7 %all-to-all-start.2 = ((bf16[64,144,128]{2,1,0:T(8,128)(2,1)}), bf16[64,144,128]{2,1,0:T(8,128)(2,1)S(1)}, u32[]{:S(2)}, u32[]{:S(2)}) async-start(bf16[64,144,128]{2,1,0:T(8,128)(2,1)} %reshape_reshape.3), calls=%async_computation.2 | async-start | bytes 4718592 | tf_op jit(solution)/shard_map/all_to_all | solution.py:45
  288.1 4.9 %fusion.23 = bf16[384,1024]{1,0:T(8,128)(2,1)} fusion(bf16[144,8,8,128]{3,2,1,0:T(8,128)(2,1)} %bitcast.69, f32[1152,768]{0,1:T(8,128)} %fusion.7), kind=kOutput, calls=%fused_computation.33 | convolution fusion | flops 909017088 | bytes 6684672 | tf_op jit(solution)/shard_map/dot_general | solution.py:31
  293.2 5.6 %fusion.18 = bf16[1024,768]{1,0:T(8,128)(2,1)} fusion(bf16[144,8,8,128]{3,2,1,0:T(8,128)(2,1)} %bitcast.67, bf16[1152,384]{0,1:T(8,128)(2,1)} %copy-done.6, bf16[1152,384]{0,1:T(8,128)(2,1)} %copy-done.5), kind=kOutput, calls=%fused_computation.30 | convolution fusion | flops 1816264704 | bytes 5701632 | tf_op jit(solution)/shard_map/dot_general | solution.py:31
  298.8 33.1 %reduce-scatter.5.cloned.1.call-done = bf16[48,1024]{1,0:T(8,128)(2,1)} async-done(((bf16[384,1024]{1,0:T(8,128)(2,1)}), bf16[48,1024]{1,0:T(8,128)(2,1)}) %reduce-scatter.5.cloned.1.call-update) | async-done | bytes 98320 | tf_op jit(solution)/shard_map/reduce_scatter | solution.py:111
  331.9 1.6 bitcast_convert_fusion.1
  333.5 41.7 %reduce-scatter.3.cloned.1.call-done = bf16[128,768]{1,0:T(8,128)(2,1)} async-done(((bf16[1024,768]{1,0:T(8,128)(2,1)}), bf16[128,768]{1,0:T(8,128)(2,1)}) %reduce-scatter.3.cloned.1.call-update) | async-done | bytes 196624 | tf_op jit(solution)/shard_map/reduce_scatter | solution.py:105
  375.3 1.7 bitcast_convert_fusion
  377.0 20.0 %all-to-all-done.2 = bf16[64,144,128]{2,1,0:T(8,128)(2,1)S(1)} async-done(((bf16[64,144,128]{2,1,0:T(8,128)(2,1)}), bf16[64,144,128]{2,1,0:T(8,128)(2,1)S(1)}, u32[]{:S(2)}, u32[]{:S(2)}) %all-to-all-start.2) | async-done | bytes 2359328 | tf_op jit(solution)/shard_map/all_to_all | solution.py:45
  397.0 2.8 copy.24
  399.7 4.2 %fusion.26 = f32[128,1024]{0,1:S(1)} fusion(bf16[1152,1024]{0,1:T(8,128)(2,1)} %bitcast.65, s32[1024]{0:T(1024)S(1)} %get-tuple-element.17, s32[1024]{0:T(1024)S(1)} %get-tuple-element.16), kind=kOutput, calls=%fused_computation.34 | convolution fusion | flops 605437952 | bytes 2891776
  404.0 0.9 copy.25
  (52 shorter events, 11.2 us)
Async XLA Ops:
  7.2 5.3 %copy-start.2 = (bf16[128,1024]{1,0:T(8,128)(2,1)S(1)}, bf16[128,1024]{1,0:T(8,128)(2,1)}, u32[]{:S(2)}) copy-start(bf16[128,1024]{1,0:T(8,128)(2,1)} %param.6) | copy-start | bytes 786436
  7.2 5.4 %copy-start.3 = (bf16[128,1024]{1,0:T(8,128)(2,1)S(1)}, bf16[128,1024]{1,0:T(8,128)(2,1)}, u32[]{:S(2)}) copy-start(bf16[128,1024]{1,0:T(8,128)(2,1)} %param.7) | copy-start | bytes 786436
  23.8 19.4 %copy-start = (bf16[1,48,1024]{2,1,0:T(8,128)(2,1)S(1)}, bf16[1,48,1024]{2,1,0:T(8,128)(2,1)}, u32[]{:S(2)}) copy-start(bf16[1,48,1024]{2,1,0:T(8,128)(2,1)} %param.11) | copy-start | bytes 294916
  23.8 227.9 %all-to-all-start = ((bf16[64,288,128]{2,1,0:T(8,128)(2,1)}), bf16[64,288,128]{2,1,0:T(8,128)(2,1)}, u32[]{:S(2)}, u32[]{:S(2)}) async-start(bf16[64,288,128]{2,1,0:T(8,128)(2,1)} %fusion), calls=%async_computation | async-start | bytes 9437184 | tf_op jit(solution)/shard_map/all_to_all | solution.py:45
  42.5 217.2 %all-gather.3.cloned.1.call-start = ((), (), s32[]{:S(2)}) async-start(), calls=%async_computation.7 | async-start | bytes 1769472 | tf_op jit(solution)/shard_map/all_gather | solution.py:95
  251.7 17.4 %all-to-all-start.1 = ((bf16[8,48,1024]{2,1,0:T(8,128)(2,1)}), bf16[8,48,1024]{2,1,0:T(8,128)(2,1)S(1)}, u32[]{:S(2)}, u32[]{:S(2)}) async-start(bf16[8,48,1024]{2,1,0:T(8,128)(2,1)} %bitcast.5), calls=%async_computation.1 | async-start | bytes 1572864 | tf_op jit(solution)/shard_map/all_to_all | solution.py:9
  259.6 6.4 %copy-start.1 = (bf16[1152,8,128]{2,1,0:T(8,128)(2,1)}, bf16[1152,8,128]{2,1,0:T(8,128)(2,1)S(1)}, u32[]{:S(2)}) copy-start(bf16[1152,8,128]{2,1,0:T(8,128)(2,1)S(1)} %get-tuple-element.14) | copy-start | bytes 7077892
  269.2 5.7 %copy-start.4 = (bf16[1,1024,768]{2,1,0:T(8,128)(2,1)S(1)}, bf16[1,1024,768]{2,1,0:T(8,128)(2,1)}, u32[]{:S(2)}) copy-start(bf16[1,1024,768]{2,1,0:T(8,128)(2,1)} %all-gather.3.cloned.1.call-done) | copy-start | bytes 4718596
  273.6 0.9 copy-start.5
  273.6 1.2 copy-start.6
  279.4 117.6 %all-to-all-start.2 = ((bf16[64,144,128]{2,1,0:T(8,128)(2,1)}), bf16[64,144,128]{2,1,0:T(8,128)(2,1)S(1)}, u32[]{:S(2)}, u32[]{:S(2)}) async-start(bf16[64,144,128]{2,1,0:T(8,128)(2,1)} %reshape_reshape.3), calls=%async_computation.2 | async-start | bytes 4718592 | tf_op jit(solution)/shard_map/all_to_all | solution.py:45
  288.0 43.9 %reduce-scatter.5.cloned.1.call-start = ((), (), s32[]{:S(2)}) async-start(), calls=%async_computation.6 | async-start | bytes 884736 | tf_op jit(solution)/shard_map/reduce_scatter | solution.py:111
  293.0 82.3 %reduce-scatter.3.cloned.1.call-start = ((), (), s32[]{:S(2)}) async-start(), calls=%async_computation.5 | async-start | bytes 1769472 | tf_op jit(solution)/shard_map/reduce_scatter | solution.py:105
Sparse Core Ops, SparseCore 0:
  45.4 32.7 all-gather.2
  293.1 38.8 reduce-scatter.4
  334.8 40.4 reduce-scatter.2
